TPU v7x, 256 devices: a whole 4x4x8 slice. The times are simulated.
256 devices in a mesh: path: 64 (over z, x, core), rep: 4 (over y).
Axes of the slice: x: 4, y: 4, z: 8, core: 2. Of those that a mesh axis runs over, the one named last changes fastest.
Arguments:
- start_state: float32 [32, 65536], P(None, 'path'), may hold values from -1.8 to 1.8
- increments: float32 [2, 32, 65536], P(None, None, 'path'), may hold values from -6 to 6
- vol_factor: float32 [32, 32], replicated, may hold values from -0.3 to 0.3
- quad_dirs: float32 [223, 32], replicated, may hold values from -1.5 to 1.5
- bundle_ids: int32 [2, 65536, 1], P(None, 'path'), may hold values from 0 to 255; in each aligned block of 1024 rows (0 to 1023, 1024 to 2047, ..., all dimensions but the last counted through in order) at most 8 rows name the same one
- bundle_slot: int32 [256], replicated, may hold values from 0 to 255, each once
Outputs:
- values: float32 [2, 65536], P(None, 'path')
- coefficients: float32 [2, 256, 256], P(None, 'path', 'rep')
Inputs may be any that keep to these rules, and one draw needn't show every extreme that they name: `bundle_ids`: at each date, no bundle id appears more than 8 times among the paths of one device; in every draw some device holds exactly 8 paths of one bundle. A permutation: bundle b sits at slot bundle_slot[b], and slot s belongs to the owner s // 4 along path.
All inputs are finite; a program needn't handle non-finite values.
Results may differ from a plain program's by a relative error of at most 0.0003.
Values sent between devices are 32-bit elements; how exact they have to be, the bound alone decides.
No kernel may reach another device: no remote copies, remote signals or barrier semaphores. Data moves between devices by JAX's collectives and lax.ppermute only.
A program may use at most 64 MiB of HBM per device.

v0:
```python
import jax
import jax.numpy as jnp
from jax import lax
from jax.sharding import PartitionSpec as P

BASIS = 256
MOST = 8

RIDGE_TERM = 32.0
DISCOUNT = 0.97
NOTIONAL = 10.0
HIGHEST = lax.Precision.HIGHEST


def exercise_value(states):
    return NOTIONAL * jnp.maximum(jnp.mean(jnp.exp(states), axis=0) - 1.0, 0.0)


def exercise_rows(states):
    return NOTIONAL * jnp.maximum(jnp.mean(jnp.exp(states), axis=1) - 1.0, 0.0)


def routing(bundle_of, bundle_slot, rep_index, reps):
    path_count = bundle_of.shape[0]
    bundles = bundle_slot.shape[0]
    labels = lax.broadcasted_iota(jnp.int32, (path_count, bundles), 1)
    slot_of = jnp.sum(jnp.where(bundle_of[:, None] == labels, bundle_slot[None, :], 0), axis=1)
    owners = bundles // reps
    later = lax.broadcasted_iota(jnp.int32, (path_count, path_count), 0)
    earlier = lax.broadcasted_iota(jnp.int32, (path_count, path_count), 1)
    same = (slot_of[:, None] == slot_of[None, :]) & (earlier < later)
    rank = jnp.sum(same.astype(jnp.int32), axis=1)
    mine = (slot_of % reps) == rep_index
    position = jnp.where(mine, (slot_of // reps) * MOST + rank, -1)
    places = lax.broadcasted_iota(jnp.int32, (owners * MOST, path_count), 0)
    forward = (places == position[None, :]).astype(jnp.float32)
    slot_rows = lax.broadcasted_iota(jnp.int32, (bundles, path_count), 0)
    slots = (slot_rows == slot_of[None, :]).astype(jnp.float32)
    return forward, slots, rank, slot_of


def send_rows(onehot, rows):
    return lax.dot_general(onehot, rows, (((1,), (1,)), ((), ())), precision=HIGHEST,
                           preferred_element_type=jnp.float32)


def exchange(block, owners):
    shaped = block.reshape((owners, MOST) + block.shape[1:])
    arrived = lax.all_to_all(shaped, "path", 0, 0, tiled=True)
    return arrived.reshape(block.shape)


def features_of(present, states, quad_dirs):
    projected = lax.dot_general(states, quad_dirs, (((1,), (1,)), ((), ())), precision=HIGHEST,
                                preferred_element_type=jnp.float32)
    return jnp.concatenate([present, states, projected * projected], axis=1)


def moments_of(states, quad_dirs, offsets):
    projected = lax.dot_general(states, quad_dirs, (((1,), (1,)), ((), ())), precision=HIGHEST,
                                preferred_element_type=jnp.float32)
    constant = jnp.ones((states.shape[0], 1), jnp.float32)
    return jnp.concatenate([constant, states, projected * projected + offsets[None, :]], axis=1)


def factor_gram(features):
    gram = lax.dot_general(features, features, (((0,), (0,)), ((), ())), precision=HIGHEST,
                           preferred_element_type=jnp.float32)
    gram = gram + RIDGE_TERM * jnp.eye(BASIS, dtype=jnp.float32)
    half = BASIS // 2
    identity = jnp.eye(half, dtype=jnp.float32)
    side = gram[half:, :half]
    corner = gram[half:, half:]

    def step(index, carry):
        block, inverses, below = carry
        factor = jnp.linalg.cholesky(block)
        inverse = lax.linalg.triangular_solve(factor, identity, left_side=True, lower=True)
        inverses = lax.dynamic_update_index_in_dim(inverses, inverse, index, 0)
        below = jnp.where(index == 0, lax.dot_general(side, inverse, (((1,), (1,)), ((), ())), precision=HIGHEST,
                                                      preferred_element_type=jnp.float32), below)
        block = corner - lax.dot_general(below, below, (((1,), (1,)), ((), ())), precision=HIGHEST,
                                         preferred_element_type=jnp.float32)
        return block, inverses, below

    start = (gram[:half, :half], jnp.zeros((2, half, half), jnp.float32), jnp.zeros((half, half), jnp.float32))
    _, inverses, below = lax.fori_loop(0, 2, step, start)
    return inverses[0], below, inverses[1]


def matvec(matrix, vector, transpose=False):
    dims = (((0,), (0,)), ((), ())) if transpose else (((1,), (0,)), ((), ()))
    return lax.dot_general(matrix, vector, dims, precision=HIGHEST, preferred_element_type=jnp.float32)


def solve_weights(factor, features, values):
    upper_inverse, below, lower_inverse = factor
    half = BASIS // 2
    right_side = lax.dot_general(features, values, (((0,), (0,)), ((), ())), precision=HIGHEST,
                                 preferred_element_type=jnp.float32)
    first = matvec(upper_inverse, right_side[:half])
    second = matvec(lower_inverse, right_side[half:] - matvec(below, first))
    second = matvec(lower_inverse, second, transpose=True)
    first = matvec(upper_inverse, first - matvec(below, second, transpose=True), transpose=True)
    return jnp.concatenate([first, second])


def new_values(weights, current, quad_dirs, offsets):
    moments = moments_of(current, quad_dirs, offsets)
    carried = jnp.dot(moments, weights, precision=HIGHEST, preferred_element_type=jnp.float32)
    return jnp.maximum(exercise_rows(current), DISCOUNT * carried)


def go_home(owner_values, weights, slots, rank, owners, reps):
    width = BASIS // reps
    dates = len(owner_values)
    per_home = [jnp.broadcast_to(v.reshape(owners, 1, MOST), (owners, reps, MOST)) for v in owner_values]
    blocks = jnp.broadcast_to(weights.reshape(1, reps, width), (owners, reps, width))
    message = jnp.concatenate(per_home + [blocks], axis=2).reshape(owners * reps, dates * MOST + width)
    arrived = lax.all_to_all(message, ("path", "rep"), 0, 0, tiled=True)
    values = []
    for d in range(dates):
        by_slot = arrived[:, d * MOST:(d + 1) * MOST]
        picked = lax.dot_general(by_slot, slots[d], (((0,), (0,)), ((), ())), precision=HIGHEST,
                                 preferred_element_type=jnp.float32)
        ranks = lax.broadcasted_iota(jnp.int32, picked.shape, 0)
        values.append(jnp.sum(jnp.where(ranks == rank[d][None, :], picked, 0.0), axis=0))
    mine = lax.dynamic_index_in_dim(arrived.reshape(owners, reps, -1), lax.axis_index("path"), 0, False)
    return values, mine[:, dates * MOST:]


def body(start_state, increments, vol_factor, quad_dirs, bundle_ids, bundle_slot):
    reps = lax.axis_size("rep")
    owners = bundle_slot.shape[0] // reps
    rep_index = lax.axis_index("rep")
    middle = start_state + jnp.dot(
        vol_factor, increments[0], precision=HIGHEST, preferred_element_type=jnp.float32
    )
    final = middle + jnp.dot(
        vol_factor, increments[1], precision=HIGHEST, preferred_element_type=jnp.float32
    )
    mixed = jnp.dot(quad_dirs, vol_factor, precision=HIGHEST, preferred_element_type=jnp.float32)
    offsets = jnp.sum(mixed * mixed, axis=1)
    assets = start_state.shape[0]
    ones = jnp.ones((1, start_state.shape[1]), jnp.float32)

    late_map, late_slots, late_rank, late_slot_of = routing(bundle_ids[0, :, 0], bundle_slot, rep_index, reps)
    early_map, early_slots, early_rank, _ = routing(bundle_ids[1, :, 0], bundle_slot, rep_index, reps)

    late_label = late_slot_of.astype(jnp.float32)[None, :]
    outgoing = jnp.concatenate(
        [send_rows(late_map, jnp.concatenate([ones, middle, final], axis=0)),
         send_rows(early_map, jnp.concatenate([ones, start_state, middle, late_label], axis=0))], axis=1)
    arrived = exchange(outgoing, owners)
    width = 1 + 2 * assets

    late_rows = arrived[:, :width]
    present = late_rows[:, :1]
    current = late_rows[:, 1:1 + assets]
    following = late_rows[:, 1 + assets:]
    late_features = features_of(present, following, quad_dirs)
    late_factor = factor_gram(late_features)
    late_weights = solve_weights(late_factor, late_features, exercise_rows(following))
    late_owner_values = new_values(late_weights, current, quad_dirs, offsets)
    copies = jnp.broadcast_to(late_weights[None, :], (owners * reps, BASIS))
    late_table = lax.all_to_all(copies, ("path", "rep"), 0, 0, tiled=True)

    early_rows = arrived[:, width:]
    present = early_rows[:, :1]
    current = early_rows[:, 1:1 + assets]
    following = early_rows[:, 1 + assets:1 + 2 * assets]
    late_slot_here = early_rows[:, 1 + 2 * assets].astype(jnp.int32)
    early_features = features_of(present, following, quad_dirs)
    early_factor = factor_gram(early_features)
    table_rows = lax.broadcasted_iota(jnp.int32, (late_slot_here.shape[0], late_table.shape[0]), 1)
    chooser = (table_rows == late_slot_here[:, None]).astype(jnp.float32)
    chosen = jnp.dot(chooser, late_table, precision=HIGHEST, preferred_element_type=jnp.float32)
    moments = moments_of(following, quad_dirs, offsets)
    carried = jnp.sum(moments * chosen, axis=1)
    early_targets = jnp.maximum(exercise_rows(following), DISCOUNT * carried)
    early_weights = solve_weights(early_factor, early_features, early_targets)
    early_owner_values = new_values(early_weights, current, quad_dirs, offsets)

    (value_middle, value_start), early_block = go_home(
        [late_owner_values, early_owner_values], early_weights,
        [late_slots, early_slots], [late_rank, early_rank], owners, reps)
    width = BASIS // reps
    late_block = lax.dynamic_slice(
        late_table, (lax.axis_index("path") * reps, rep_index * width), (reps, width))
    return (jnp.stack([value_middle, value_start]), jnp.stack([late_block, early_block]))


def solution(mesh):
    placed = (P(None, "path"), P(None, None, "path"), P(), P(), P(None, "path", None), P())
    return jax.shard_map(
        body,
        mesh=mesh,
        in_specs=placed,
        out_specs=(P(None, "path"), P(None, "path", "rep")),
        check_vma=False,
    )
```

profile of v0, /device:TPU:8, one launch (start us, length us, event | category | flops | bytes accessed | tf_op | source)
XLA Modules:
  0.0 187.2 jit_solution(465104734464072693)
XLA Ops:
  0.7 0.8 fusion.136
  1.4 1.6 select_reduce_fusion.3
  3.1 2.4 %convert_reduce_fusion = (s32[1024]{0:T(1024)S(1)}, s32[1024]{0:T(1024)S(1)}) fusion(s32[1024]{0:T(1024)S(1)} %get-tuple-element.305, s32[1024]{0:T(1024)S(1)} %get-tuple-element.304), kind=kLoop, calls=%fused_computation.32 | loop fusion | flops 9435136 | bytes 16384 | tf_op jit(solution)/shard_map/reduce_sum | solution.py:32
  5.5 1.2 convolution_add_fusion.3
  6.8 0.2 convolution_add_fusion.2
  7.1 1.2 fusion.21
  8.3 1.2 fusion.20
  9.5 1.0 copy.39
  10.5 12.1 %all-to-all-start = ((f32[64,8,131]{2,1,0:T(8,128)}), f32[64,8,131]{2,1,0:T(8,128)S(1)}, u32[]{:S(2)}, u32[]{:S(2)}) async-start(f32[64,8,131]{2,1,0:T(8,128)} %bitcast.5), calls=%async_computation | async-start | bytes 1048576 | tf_op jit(solution)/shard_map/all_to_all | solution.py:49
  22.7 0.2 fusion.27
  22.9 17.2 %all-to-all-done = f32[64,8,131]{2,1,0:T(8,128)S(1)} async-done(((f32[64,8,131]{2,1,0:T(8,128)}), f32[64,8,131]{2,1,0:T(8,128)S(1)}, u32[]{:S(2)}, u32[]{:S(2)}) %all-to-all-start) | async-done | bytes 268320 | tf_op jit(solution)/shard_map/all_to_all | solution.py:49
  40.1 0.3 fusion.132
  40.5 1.4 convolution_multiply_fusion.2
  42.0 0.7 fusion.22
  42.6 1.4 broadcast_add_fusion
  44.3 1.9 %convolution_add_fusion.1 = f32[256,256]{1,0:T(8,128)S(1)} fusion(f32[512,223]{0,1:T(8,128)} %convolution_multiply_fusion.2, f32[512,32]{0,1:T(8,128)S(1)} %copy.49, f32[512,1]{0,1:T(1,128)S(1)} %copy.48), kind=kOutput, calls=%fused_computation.50 | convolution fusion | flops 403111936 | bytes 786432 | tf_op jit(solution)/shard_map/dot_general | solution.py:67
  46.2 0.5 fusion.52
  46.8 47.9 %while.36 = (s32[]{:T(128)}, f32[128,128]{1,0:T(8,128)S(1)}, f32[2,128,128]{2,1,0:T(8,128)S(1)}, f32[128,128]{0,1:T(8,128)S(1)}, f32[128,128]{1,0:T(8,128)S(1)},...) while((s32[]{:T(128)}, f32[128,128]{1,0:T(8,128)S(1)}, f32[2,128,128]{2,1,0:T(8,128)S(1)}, ...), condition=%wide.region_9.12_spmd.clone, body=%wide.region_6.11_spmd.clone.sunk | while | flops 75726976 | bytes 1180773 | solution.py:87
  46.9 11.7 %cholesky.155 = f32[128,128]{1,0:T(8,128)S(1)} custom-call(f32[128,128]{1,0:T(8,128)S(1)} %fusion.185), custom_call_target="Cholesky" | custom-call | tf_op jit(solution)/shard_map/while/body/eval_jaxpr/jit(cholesky)/cholesky | solution.py:77
  58.7 0.7 compare_reduce_fusion.4
  59.4 0.7 fusion.186
  60.1 9.8 %custom-call.12 = f32[1,128,128]{1,2,0:T(8,128)S(1)} custom-call(f32[1,128,128]{2,1,0:T(8,128)S(1)} %fusion.186), custom_call_target="InvertDiagBlocksLowerTriangular" | custom-call | tf_op jit(solution)/shard_map/while/body/eval_jaxpr/triangular_solve/custom-call.0 | solution.py:78
  69.9 0.3 bitcast_dynamic-update-slice_fusion.4
  70.2 0.3 fusion.187
  70.5 0.3 convolution_subtract_fusion.4
  70.9 11.7 %cholesky.155 = f32[128,128]{1,0:T(8,128)S(1)} custom-call(f32[128,128]{1,0:T(8,128)S(1)} %fusion.185), custom_call_target="Cholesky" | custom-call | tf_op jit(solution)/shard_map/while/body/eval_jaxpr/jit(cholesky)/cholesky | solution.py:77
  82.6 0.7 compare_reduce_fusion.4
  83.4 0.7 fusion.186
  84.0 9.8 %custom-call.12 = f32[1,128,128]{1,2,0:T(8,128)S(1)} custom-call(f32[1,128,128]{2,1,0:T(8,128)S(1)} %fusion.186), custom_call_target="InvertDiagBlocksLowerTriangular" | custom-call | tf_op jit(solution)/shard_map/while/body/eval_jaxpr/triangular_solve/custom-call.0 | solution.py:78
  93.9 0.3 bitcast_dynamic-update-slice_fusion.4
  94.2 0.3 fusion.187
  94.4 0.3 convolution_subtract_fusion.4
  94.9 0.2 fusion.35
  96.1 0.8 broadcast_in_dim.90
  96.9 8.4 %all-to-all-start.1 = ((f32[256,1,256]{2,1,0:T(1,128)}), f32[256,1,256]{2,1,0:T(1,128)S(1)}, u32[]{:S(2)}, u32[]{:S(2)}) async-start(f32[256,1,256]{2,1,0:T(1,128)} %broadcast_in_dim.90), calls=%async_computation.1 | async-start | bytes 524288 | tf_op jit(solution)/shard_map/all_to_all | solution.py:166
  105.6 0.7 convolution_add_fusion
  106.3 47.7 %while.37 = (s32[]{:T(128)}, f32[128,128]{1,0:T(8,128)S(1)}, f32[2,128,128]{2,1,0:T(8,128)S(1)}, f32[128,128]{0,1:T(8,128)S(1)}, f32[128,128]{1,0:T(8,128)S(1)},...) while((s32[]{:T(128)}, f32[128,128]{1,0:T(8,128)S(1)}, f32[2,128,128]{2,1,0:T(8,128)S(1)}, ...), condition=%wide.region_13.16_spmd.clone, body=%wide.region_12.15_spmd.clone.sunk | while | flops 75726976 | bytes 1180773 | solution.py:87
  106.4 11.7 %cholesky.169 = f32[128,128]{1,0:T(8,128)S(1)} custom-call(f32[128,128]{1,0:T(8,128)S(1)} %fusion.192), custom_call_target="Cholesky" | custom-call | tf_op jit(solution)/shard_map/while/body/eval_jaxpr/jit(cholesky)/cholesky | solution.py:77
  118.2 0.6 compare_reduce_fusion.5
  118.8 0.7 fusion.193
  119.5 9.8 %custom-call.13 = f32[1,128,128]{1,2,0:T(8,128)S(1)} custom-call(f32[1,128,128]{2,1,0:T(8,128)S(1)} %fusion.193), custom_call_target="InvertDiagBlocksLowerTriangular" | custom-call | tf_op jit(solution)/shard_map/while/body/eval_jaxpr/triangular_solve/custom-call.0 | solution.py:78
  129.3 0.3 bitcast_dynamic-update-slice_fusion.5
  129.6 0.3 fusion.194
  129.9 0.3 convolution_subtract_fusion.5
  130.3 11.7 %cholesky.169 = f32[128,128]{1,0:T(8,128)S(1)} custom-call(f32[128,128]{1,0:T(8,128)S(1)} %fusion.192), custom_call_target="Cholesky" | custom-call | tf_op jit(solution)/shard_map/while/body/eval_jaxpr/jit(cholesky)/cholesky | solution.py:77
  142.0 0.6 compare_reduce_fusion.5
  142.7 0.7 fusion.193
  143.3 9.8 %custom-call.13 = f32[1,128,128]{1,2,0:T(8,128)S(1)} custom-call(f32[1,128,128]{2,1,0:T(8,128)S(1)} %fusion.193), custom_call_target="InvertDiagBlocksLowerTriangular" | custom-call | tf_op jit(solution)/shard_map/while/body/eval_jaxpr/triangular_solve/custom-call.0 | solution.py:78
  153.2 0.3 bitcast_dynamic-update-slice_fusion.5
  153.5 0.3 fusion.194
  153.7 0.3 convolution_subtract_fusion.5
  154.0 0.5 fusion.40
  154.8 0.2 fusion.68
  155.1 0.7 fusion.23
  155.8 0.5 fusion.24
  156.4 0.5 fusion.53
  158.3 0.5 fusion.45
  159.0 0.8 pad_maximum_fusion.6
  159.8 13.7 %all-to-all-start.2 = ((f32[256,1,80]{2,1,0:T(1,128)}), f32[256,1,80]{2,1,0:T(1,128)S(1)}, u32[]{:S(2)}, u32[]{:S(2)}) async-start(f32[256,1,80]{2,1,0:T(1,128)} %bitcast.43), calls=%async_computation.2 | async-start | bytes 262144 | tf_op jit(solution)/shard_map/all_to_all | solution.py:120
  173.7 11.3 %all-to-all-done.2 = f32[256,1,80]{2,1,0:T(1,128)S(1)} async-done(((f32[256,1,80]{2,1,0:T(1,128)}), f32[256,1,80]{2,1,0:T(1,128)S(1)}, u32[]{:S(2)}, u32[]{:S(2)}) %all-to-all-start.2) | async-done | bytes 81952 | tf_op jit(solution)/shard_map/all_to_all | solution.py:120
  185.0 0.4 fusion.25
  185.4 0.5 fusion.26
  186.0 0.6 pad_maximum_fusion.8
  186.6 0.6 pad_maximum_fusion.7
  (75 shorter events, 4.5 us)
Async XLA Ops:
  0.6 22.0 %copy-start = (f32[223,32]{0,1:T(8,128)S(1)}, f32[223,32]{0,1:T(8,128)}, u32[]{:S(2)}) copy-start(f32[223,32]{0,1:T(8,128)} %param.16) | copy-start | bytes 85636
  0.6 6.4 %copy-start.4 = (f32[32,1024]{1,0:T(8,128)S(1)}, f32[32,1024]{1,0:T(8,128)}, u32[]{:S(2)}) copy-start(f32[32,1024]{1,0:T(8,128)} %param.13) | copy-start | bytes 393220
  0.7 6.1 %copy-start.3 = (f32[2,32,1024]{2,1,0:T(8,128)S(1)}, f32[2,32,1024]{2,1,0:T(8,128)}, u32[]{:S(2)}) copy-start(f32[2,32,1024]{2,1,0:T(8,128)} %param.14) | copy-start | bytes 786436
  0.7 6.1 %copy-start.5 = (f32[32,32]{1,0:T(8,128)S(1)}, f32[32,32]{1,0:T(8,128)}, u32[]{:S(2)}) copy-start(f32[32,32]{1,0:T(8,128)} %param.15) | copy-start | bytes 12292
  10.5 29.6 %all-to-all-start = ((f32[64,8,131]{2,1,0:T(8,128)}), f32[64,8,131]{2,1,0:T(8,128)S(1)}, u32[]{:S(2)}, u32[]{:S(2)}) async-start(f32[64,8,131]{2,1,0:T(8,128)} %bitcast.5), calls=%async_computation | async-start | bytes 1048576 | tf_op jit(solution)/shard_map/all_to_all | solution.py:49
  44.3 1.9 %copy-start.2 = (f32[512,223]{0,1:T(8,128)S(1)}, f32[512,223]{0,1:T(8,128)}, u32[]{:S(2)}) copy-start(f32[512,223]{0,1:T(8,128)} %convolution_multiply_fusion.2) | copy-start | bytes 1370116
  96.9 58.8 %all-to-all-start.1 = ((f32[256,1,256]{2,1,0:T(1,128)}), f32[256,1,256]{2,1,0:T(1,128)S(1)}, u32[]{:S(2)}, u32[]{:S(2)}) async-start(f32[256,1,256]{2,1,0:T(1,128)} %broadcast_in_dim.90), calls=%async_computation.1 | async-start | bytes 524288 | tf_op jit(solution)/shard_map/all_to_all | solution.py:166
  154.8 1.0 copy-start.1
  159.8 25.1 %all-to-all-start.2 = ((f32[256,1,80]{2,1,0:T(1,128)}), f32[256,1,80]{2,1,0:T(1,128)S(1)}, u32[]{:S(2)}, u32[]{:S(2)}) async-start(f32[256,1,80]{2,1,0:T(1,128)} %bitcast.43), calls=%async_computation.2 | async-start | bytes 262144 | tf_op jit(solution)/shard_map/all_to_all | solution.py:120
where the time goes:
time: 190 us; the launch traced here: 187 us
  other arithmetic  98.2 us (52%)
  starting transfers between devices  34.3 us (18%)
  waiting for transfers between devices  28.5 us (15%)
  matrix products  20.1 us (11%)
  local copies, waits for them, and re-layouts  4.84 us (3%)
    another operation x12, other arithmetic, step(): factor = jnp.linalg.cholesky(block)  49.7 us
    another operation x8, other arithmetic, step(): lax.linalg.triangular_solve(factor, identity, left_side=True, lower=True)  41.9 us
    all_to_all x1, waiting for transfers between devices, exchange(): arrived = lax.all_to_all(shaped, 'path', 0, 0, tiled=True)  17.2 us
    all_to_all x1, starting transfers between devices, go_home(): arrived = lax.all_to_all(message, ('path', 'rep'), 0, 0, tiled=True)  13.7 us
    all_to_all x1, starting transfers between devices, exchange(): arrived = lax.all_to_all(shaped, 'path', 0, 0, tiled=True)  12.1 us
    all_to_all x1, waiting for transfers between devices, go_home(): arrived = lax.all_to_all(message, ('path', 'rep'), 0, 0, tiled=True)  11.3 us
    all_to_all x1, starting transfers between devices, body(): late_table = lax.all_to_all(copies, ('path', 'rep'), 0, 0, tiled=True)  8.43 us
  transfers between devices with their start and end apart: 3, of which 2 were waited for; matrix products, arithmetic and copies ran while one was open for 27% of the time, Pallas kernels for 0%

commit v1 on v0

--- a/solution.py
+++ b/solution.py
@@ -45,7 +45,7 @@
 
 
 def exchange(block, owners):
-    shaped = block.reshape((owners, MOST) + block.shape[1:])
+    shaped = block.reshape(owners, -1)
     arrived = lax.all_to_all(shaped, "path", 0, 0, tiled=True)
     return arrived.reshape(block.shape)
 

time: 190 us -> 187 us (0.984)
  waiting for transfers between devices: 28.5 us -> 24.3 us
    all_to_all x1, waiting for transfers between devices: 17.2 us -> 13 us  [exchange(): arrived = lax.all_to_all(shaped, 'path', 0, 0, tiled=True)]
where the time goes in v1:
time: 187 us; the launch traced here: 184 us
  other arithmetic  98.9 us (53%)
  starting transfers between devices  33.6 us (18%)
  waiting for transfers between devices  24.3 us (13%)
  matrix products  20.1 us (11%)
  local copies, waits for them, and re-layouts  5.69 us (3%)
    another operation x12, other arithmetic, step(): factor = jnp.linalg.cholesky(block)  49.7 us
    another operation x8, other arithmetic, step(): lax.linalg.triangular_solve(factor, identity, left_side=True, lower=True)  41.9 us
    all_to_all x1, starting transfers between devices, go_home(): arrived = lax.all_to_all(message, ('path', 'rep'), 0, 0, tiled=True)  13.7 us
    all_to_all x1, waiting for transfers between devices, exchange(): arrived = lax.all_to_all(shaped, 'path', 0, 0, tiled=True)  13 us
    all_to_all x1, starting transfers between devices, exchange(): arrived = lax.all_to_all(shaped, 'path', 0, 0, tiled=True)  12.1 us
    all_to_all x1, waiting for transfers between devices, go_home(): arrived = lax.all_to_all(message, ('path', 'rep'), 0, 0, tiled=True)  11.3 us
    all_to_all x1, starting transfers between devices, body(): late_table = lax.all_to_all(copies, ('path', 'rep'), 0, 0, tiled=True)  7.8 us
  transfers between devices with their start and end apart: 3, of which 2 were waited for; matrix products, arithmetic and copies ran while one was open for 27% of the time, Pallas kernels for 0%

profile of v1, /device:TPU:8, one launch (start us, length us, event | category | flops | bytes accessed | tf_op | source)
XLA Modules:
  0.0 183.9 jit_solution(10500737592759362652)
XLA Ops:
  0.7 0.8 fusion.136
  1.4 1.6 select_reduce_fusion.3
  3.1 2.4 %convert_reduce_fusion = (s32[1024]{0:T(1024)S(1)}, s32[1024]{0:T(1024)S(1)}) fusion(s32[1024]{0:T(1024)S(1)} %get-tuple-element.305, s32[1024]{0:T(1024)S(1)} %get-tuple-element.304), kind=kLoop, calls=%fused_computation.32 | loop fusion | flops 9435136 | bytes 16384 | tf_op jit(solution)/shard_map/reduce_sum | solution.py:32
  5.5 1.2 convolution_add_fusion.3
  6.8 0.2 convolution_add_fusion.2
  7.1 1.2 fusion.21
  8.3 1.2 fusion.20
  9.7 1.3 all_to_all.27
  11.0 12.1 %all-to-all-start = ((f32[64,1,1048]{2,1,0:T(1,128)}), f32[64,1,1048]{2,1,0:T(1,128)S(1)}, u32[]{:S(2)}, u32[]{:S(2)}) async-start(f32[64,1,1048]{2,1,0:T(1,128)} %all_to_all.27), calls=%async_computation | async-start | bytes 589824 | tf_op jit(solution)/shard_map/all_to_all | solution.py:49
  23.2 0.2 fusion.27
  23.4 13.0 %all-to-all-done = f32[64,1,1048]{2,1,0:T(1,128)S(1)} async-done(((f32[64,1,1048]{2,1,0:T(1,128)}), f32[64,1,1048]{2,1,0:T(1,128)S(1)}, u32[]{:S(2)}, u32[]{:S(2)}) %all-to-all-start) | async-done | bytes 268320 | tf_op jit(solution)/shard_map/all_to_all | solution.py:49
  36.4 0.7 reduce.4
  37.1 0.3 reshape.133
  37.4 0.3 fusion.132
  37.9 1.4 convolution_multiply_fusion.2
  39.3 0.7 fusion.22
  40.0 1.4 broadcast_add_fusion
  41.7 1.9 %convolution_add_fusion.1 = f32[256,256]{1,0:T(8,128)S(1)} fusion(f32[512,223]{0,1:T(8,128)} %convolution_multiply_fusion.2, f32[512,32]{0,1:T(8,128)S(1)} %copy.51, f32[512,1]{0,1:T(1,128)S(1)} %copy.50), kind=kOutput, calls=%fused_computation.50 | convolution fusion | flops 403111936 | bytes 786432 | tf_op jit(solution)/shard_map/dot_general | solution.py:67
  43.6 0.5 fusion.52
  44.2 47.9 %while.36 = (s32[]{:T(128)}, f32[128,128]{1,0:T(8,128)S(1)}, f32[2,128,128]{2,1,0:T(8,128)S(1)}, f32[128,128]{0,1:T(8,128)S(1)}, f32[128,128]{1,0:T(8,128)S(1)},...) while((s32[]{:T(128)}, f32[128,128]{1,0:T(8,128)S(1)}, f32[2,128,128]{2,1,0:T(8,128)S(1)}, ...), condition=%wide.region_9.12_spmd.clone, body=%wide.region_6.11_spmd.clone.sunk | while | flops 75726976 | bytes 1180773 | solution.py:87
  44.3 11.7 %cholesky.155 = f32[128,128]{1,0:T(8,128)S(1)} custom-call(f32[128,128]{1,0:T(8,128)S(1)} %fusion.185), custom_call_target="Cholesky" | custom-call | tf_op jit(solution)/shard_map/while/body/eval_jaxpr/jit(cholesky)/cholesky | solution.py:77
  56.0 0.7 compare_reduce_fusion.4
  56.7 0.7 fusion.186
  57.4 9.8 %custom-call.12 = f32[1,128,128]{1,2,0:T(8,128)S(1)} custom-call(f32[1,128,128]{2,1,0:T(8,128)S(1)} %fusion.186), custom_call_target="InvertDiagBlocksLowerTriangular" | custom-call | tf_op jit(solution)/shard_map/while/body/eval_jaxpr/triangular_solve/custom-call.0 | solution.py:78
  67.3 0.3 bitcast_dynamic-update-slice_fusion.4
  67.6 0.3 fusion.187
  67.8 0.3 convolution_subtract_fusion.4
  68.3 11.7 %cholesky.155 = f32[128,128]{1,0:T(8,128)S(1)} custom-call(f32[128,128]{1,0:T(8,128)S(1)} %fusion.185), custom_call_target="Cholesky" | custom-call | tf_op jit(solution)/shard_map/while/body/eval_jaxpr/jit(cholesky)/cholesky | solution.py:77
  80.0 0.7 compare_reduce_fusion.4
  80.7 0.7 fusion.186
  81.4 9.8 %custom-call.12 = f32[1,128,128]{1,2,0:T(8,128)S(1)} custom-call(f32[1,128,128]{2,1,0:T(8,128)S(1)} %fusion.186), custom_call_target="InvertDiagBlocksLowerTriangular" | custom-call | tf_op jit(solution)/shard_map/while/body/eval_jaxpr/triangular_solve/custom-call.0 | solution.py:78
  91.2 0.3 bitcast_dynamic-update-slice_fusion.4
  91.5 0.3 fusion.187
  91.8 0.3 convolution_subtract_fusion.4
  93.4 0.8 broadcast_in_dim.90
  94.3 7.8 %all-to-all-start.1 = ((f32[256,1,256]{2,1,0:T(1,128)}), f32[256,1,256]{2,1,0:T(1,128)S(1)}, u32[]{:S(2)}, u32[]{:S(2)}) async-start(f32[256,1,256]{2,1,0:T(1,128)} %broadcast_in_dim.90), calls=%async_computation.1 | async-start | bytes 524288 | tf_op jit(solution)/shard_map/all_to_all | solution.py:166
  102.3 0.7 convolution_add_fusion
  103.0 47.7 %while.37 = (s32[]{:T(128)}, f32[128,128]{1,0:T(8,128)S(1)}, f32[2,128,128]{2,1,0:T(8,128)S(1)}, f32[128,128]{0,1:T(8,128)S(1)}, f32[128,128]{1,0:T(8,128)S(1)},...) while((s32[]{:T(128)}, f32[128,128]{1,0:T(8,128)S(1)}, f32[2,128,128]{2,1,0:T(8,128)S(1)}, ...), condition=%wide.region_13.16_spmd.clone, body=%wide.region_12.15_spmd.clone.sunk | while | flops 75726976 | bytes 1180773 | solution.py:87
  103.1 11.7 %cholesky.169 = f32[128,128]{1,0:T(8,128)S(1)} custom-call(f32[128,128]{1,0:T(8,128)S(1)} %fusion.192), custom_call_target="Cholesky" | custom-call | tf_op jit(solution)/shard_map/while/body/eval_jaxpr/jit(cholesky)/cholesky | solution.py:77
  114.9 0.6 compare_reduce_fusion.5
  115.5 0.7 fusion.193
  116.2 9.8 %custom-call.13 = f32[1,128,128]{1,2,0:T(8,128)S(1)} custom-call(f32[1,128,128]{2,1,0:T(8,128)S(1)} %fusion.193), custom_call_target="InvertDiagBlocksLowerTriangular" | custom-call | tf_op jit(solution)/shard_map/while/body/eval_jaxpr/triangular_solve/custom-call.0 | solution.py:78
  126.0 0.3 bitcast_dynamic-update-slice_fusion.5
  126.3 0.3 fusion.194
  126.6 0.3 convolution_subtract_fusion.5
  127.0 11.7 %cholesky.169 = f32[128,128]{1,0:T(8,128)S(1)} custom-call(f32[128,128]{1,0:T(8,128)S(1)} %fusion.192), custom_call_target="Cholesky" | custom-call | tf_op jit(solution)/shard_map/while/body/eval_jaxpr/jit(cholesky)/cholesky | solution.py:77
  138.8 0.6 compare_reduce_fusion.5
  139.4 0.7 fusion.193
  140.1 9.8 %custom-call.13 = f32[1,128,128]{1,2,0:T(8,128)S(1)} custom-call(f32[1,128,128]{2,1,0:T(8,128)S(1)} %fusion.193), custom_call_target="InvertDiagBlocksLowerTriangular" | custom-call | tf_op jit(solution)/shard_map/while/body/eval_jaxpr/triangular_solve/custom-call.0 | solution.py:78
  149.9 0.3 bitcast_dynamic-update-slice_fusion.5
  150.2 0.3 fusion.194
  150.5 0.3 convolution_subtract_fusion.5
  150.8 0.5 fusion.40
  151.8 0.7 fusion.23
  152.6 0.5 fusion.24
  153.1 0.5 fusion.53
  155.0 0.5 fusion.45
  155.7 0.8 pad_maximum_fusion.6
  156.6 13.7 %all-to-all-start.2 = ((f32[256,1,80]{2,1,0:T(1,128)}), f32[256,1,80]{2,1,0:T(1,128)S(1)}, u32[]{:S(2)}, u32[]{:S(2)}) async-start(f32[256,1,80]{2,1,0:T(1,128)} %bitcast.41), calls=%async_computation.2 | async-start | bytes 262144 | tf_op jit(solution)/shard_map/all_to_all | solution.py:120
  170.4 11.3 %all-to-all-done.2 = f32[256,1,80]{2,1,0:T(1,128)S(1)} async-done(((f32[256,1,80]{2,1,0:T(1,128)}), f32[256,1,80]{2,1,0:T(1,128)S(1)}, u32[]{:S(2)}, u32[]{:S(2)}) %all-to-all-start.2) | async-done | bytes 81952 | tf_op jit(solution)/shard_map/all_to_all | solution.py:120
  181.7 0.4 fusion.25
  182.2 0.5 fusion.26
  182.7 0.6 pad_maximum_fusion.8
  183.3 0.6 pad_maximum_fusion.7
  (78 shorter events, 5.2 us)
Async XLA Ops:
  0.6 22.5 %copy-start = (f32[223,32]{0,1:T(8,128)S(1)}, f32[223,32]{0,1:T(8,128)}, u32[]{:S(2)}) copy-start(f32[223,32]{0,1:T(8,128)} %param.16) | copy-start | bytes 85636
  0.6 6.4 %copy-start.4 = (f32[32,1024]{1,0:T(8,128)S(1)}, f32[32,1024]{1,0:T(8,128)}, u32[]{:S(2)}) copy-start(f32[32,1024]{1,0:T(8,128)} %param.13) | copy-start | bytes 393220
  0.7 6.1 %copy-start.3 = (f32[2,32,1024]{2,1,0:T(8,128)S(1)}, f32[2,32,1024]{2,1,0:T(8,128)}, u32[]{:S(2)}) copy-start(f32[2,32,1024]{2,1,0:T(8,128)} %param.14) | copy-start | bytes 786436
  0.7 6.1 %copy-start.5 = (f32[32,32]{1,0:T(8,128)S(1)}, f32[32,32]{1,0:T(8,128)}, u32[]{:S(2)}) copy-start(f32[32,32]{1,0:T(8,128)} %param.15) | copy-start | bytes 12292
  11.0 25.4 %all-to-all-start = ((f32[64,1,1048]{2,1,0:T(1,128)}), f32[64,1,1048]{2,1,0:T(1,128)S(1)}, u32[]{:S(2)}, u32[]{:S(2)}) async-start(f32[64,1,1048]{2,1,0:T(1,128)} %all_to_all.27), calls=%async_computation | async-start | bytes 589824 | tf_op jit(solution)/shard_map/all_to_all | solution.py:49
  41.7 1.9 %copy-start.2 = (f32[512,223]{0,1:T(8,128)S(1)}, f32[512,223]{0,1:T(8,128)}, u32[]{:S(2)}) copy-start(f32[512,223]{0,1:T(8,128)} %convolution_multiply_fusion.2) | copy-start | bytes 1370116
  94.3 58.2 %all-to-all-start.1 = ((f32[256,1,256]{2,1,0:T(1,128)}), f32[256,1,256]{2,1,0:T(1,128)S(1)}, u32[]{:S(2)}, u32[]{:S(2)}) async-start(f32[256,1,256]{2,1,0:T(1,128)} %broadcast_in_dim.90), calls=%async_computation.1 | async-start | bytes 524288 | tf_op jit(solution)/shard_map/all_to_all | solution.py:166
  151.5 1.0 copy-start.1
  156.6 25.1 %all-to-all-start.2 = ((f32[256,1,80]{2,1,0:T(1,128)}), f32[256,1,80]{2,1,0:T(1,128)S(1)}, u32[]{:S(2)}, u32[]{:S(2)}) async-start(f32[256,1,80]{2,1,0:T(1,128)} %bitcast.41), calls=%async_computation.2 | async-start | bytes 262144 | tf_op jit(solution)/shard_map/all_to_all | solution.py:120

commit v2 on v1

--- a/solution.py
+++ b/solution.py
@@ -26,10 +26,19 @@
     labels = lax.broadcasted_iota(jnp.int32, (path_count, bundles), 1)
     slot_of = jnp.sum(jnp.where(bundle_of[:, None] == labels, bundle_slot[None, :], 0), axis=1)
     owners = bundles // reps
-    later = lax.broadcasted_iota(jnp.int32, (path_count, path_count), 0)
-    earlier = lax.broadcasted_iota(jnp.int32, (path_count, path_count), 1)
-    same = (slot_of[:, None] == slot_of[None, :]) & (earlier < later)
-    rank = jnp.sum(same.astype(jnp.int32), axis=1)
+    block = 128
+    blocks = path_count // block
+    hot = (slot_of[:, None] == lax.broadcasted_iota(jnp.int32, (path_count, bundles), 1)).astype(jnp.bfloat16)
+    hot = hot.reshape(blocks, block, bundles)
+    within = (lax.broadcasted_iota(jnp.int32, (block, block), 1)
+              < lax.broadcasted_iota(jnp.int32, (block, block), 0)).astype(jnp.bfloat16)
+    counts = jnp.einsum("pq,bqs->bps", within, hot, preferred_element_type=jnp.float32)
+    totals = jnp.sum(hot.astype(jnp.float32), axis=1)
+    before = (lax.broadcasted_iota(jnp.int32, (blocks, blocks), 1)
+              < lax.broadcasted_iota(jnp.int32, (blocks, blocks), 0)).astype(jnp.float32)
+    offsets_by_block = jnp.dot(before, totals, precision=HIGHEST, preferred_element_type=jnp.float32)
+    counts = counts + offsets_by_block[:, None, :]
+    rank = jnp.sum(counts * hot.astype(jnp.float32), axis=2).reshape(path_count).astype(jnp.int32)
     mine = (slot_of % reps) == rep_index
     position = jnp.where(mine, (slot_of // reps) * MOST + rank, -1)
     places = lax.broadcasted_iota(jnp.int32, (owners * MOST, path_count), 0)

time: 187 us -> 185 us (0.989)
  other arithmetic: 98.9 us -> 97 us
    reduce_sum x1 -> x2, other arithmetic: 2.41 us -> 0.43 us  [routing(): totals = jnp.sum(hot.astype(jnp.float32), axis=1)]
  transfers between devices with their start and end apart: 3 -> 3, of which waited for: 2 -> 2; matrix products, arithmetic and copies ran while one was open for 27% -> 28% of each run, Pallas kernels for 0% -> 0%
where the time goes in v2:
time: 185 us; the launch traced here: 183 us
  other arithmetic  97 us (52%)
  starting transfers between devices  33.6 us (18%)
  waiting for transfers between devices  24.3 us (13%)
  matrix products  20.2 us (11%)
  local copies, waits for them, and re-layouts  6.15 us (3%)
    another operation x12, other arithmetic, step(): factor = jnp.linalg.cholesky(block)  49.7 us
    another operation x8, other arithmetic, step(): lax.linalg.triangular_solve(factor, identity, left_side=True, lower=True)  41.9 us
    all_to_all x1, starting transfers between devices, go_home(): arrived = lax.all_to_all(message, ('path', 'rep'), 0, 0, tiled=True)  13.7 us
    all_to_all x1, waiting for transfers between devices, exchange(): arrived = lax.all_to_all(shaped, 'path', 0, 0, tiled=True)  12.9 us
    all_to_all x1, starting transfers between devices, exchange(): arrived = lax.all_to_all(shaped, 'path', 0, 0, tiled=True)  12.1 us
    all_to_all x1, waiting for transfers between devices, go_home(): arrived = lax.all_to_all(message, ('path', 'rep'), 0, 0, tiled=True)  11.3 us
    all_to_all x1, starting transfers between devices, body(): late_table = lax.all_to_all(copies, ('path', 'rep'), 0, 0, tiled=True)  7.8 us
  transfers between devices with their start and end apart: 3, of which 2 were waited for; matrix products, arithmetic and copies ran while one was open for 28% of the time, Pallas kernels for 0%

profile of v2, /device:TPU:8, one launch (start us, length us, event | category | flops | bytes accessed | tf_op | source)
XLA Modules:
  0.0 182.5 jit_solution(11123696569337362254)
XLA Ops:
  0.6 0.7 fusion.149
  1.4 1.6 select_reduce_fusion.3
  3.3 0.5 fusion.25
  4.2 0.5 fusion.24
  4.6 0.5 copy-done.3
  5.4 0.3 convolution_add_fusion.4
  5.7 1.2 fusion.19
  6.9 1.2 fusion.18
  8.3 1.3 all_to_all.27
  9.6 12.1 %all-to-all-start = ((f32[64,1,1048]{2,1,0:T(1,128)}), f32[64,1,1048]{2,1,0:T(1,128)S(1)}, u32[]{:S(2)}, u32[]{:S(2)}) async-start(f32[64,1,1048]{2,1,0:T(1,128)} %all_to_all.27), calls=%async_computation | async-start | bytes 589824 | tf_op jit(solution)/shard_map/all_to_all | solution.py:58
  22.0 12.9 %all-to-all-done = f32[64,1,1048]{2,1,0:T(1,128)S(1)} async-done(((f32[64,1,1048]{2,1,0:T(1,128)}), f32[64,1,1048]{2,1,0:T(1,128)S(1)}, u32[]{:S(2)}, u32[]{:S(2)}) %all-to-all-start) | async-done | bytes 268320 | tf_op jit(solution)/shard_map/all_to_all | solution.py:58
  35.0 0.7 reduce.4
  35.7 0.3 reshape.173
  36.0 0.3 fusion.145
  36.5 1.4 convolution_multiply_fusion.2
  38.0 0.7 fusion.26
  38.6 1.4 broadcast_add_fusion
  40.3 1.9 %convolution_add_fusion.3 = f32[256,256]{1,0:T(8,128)S(1)} fusion(f32[512,223]{0,1:T(8,128)} %convolution_multiply_fusion.2, f32[512,32]{0,1:T(8,128)S(1)} %copy.51, f32[512,1]{0,1:T(1,128)S(1)} %copy.50), kind=kOutput, calls=%fused_computation.55 | convolution fusion | flops 403111936 | bytes 786432 | tf_op jit(solution)/shard_map/dot_general | solution.py:76
  42.2 0.5 fusion.60
  42.8 47.9 %while.36 = (s32[]{:T(128)}, f32[128,128]{1,0:T(8,128)S(1)}, f32[2,128,128]{2,1,0:T(8,128)S(1)}, f32[128,128]{0,1:T(8,128)S(1)}, f32[128,128]{1,0:T(8,128)S(1)},...) while((s32[]{:T(128)}, f32[128,128]{1,0:T(8,128)S(1)}, f32[2,128,128]{2,1,0:T(8,128)S(1)}, ...), condition=%wide.region_11.14_spmd.clone, body=%wide.region_8.13_spmd.clone.sunk | while | flops 75726976 | bytes 1180773 | solution.py:96
  42.9 11.7 %cholesky.155 = f32[128,128]{1,0:T(8,128)S(1)} custom-call(f32[128,128]{1,0:T(8,128)S(1)} %fusion.200), custom_call_target="Cholesky" | custom-call | tf_op jit(solution)/shard_map/while/body/eval_jaxpr/jit(cholesky)/cholesky | solution.py:86
  54.7 0.7 compare_reduce_fusion.4
  55.4 0.7 fusion.201
  56.1 9.8 %custom-call.12 = f32[1,128,128]{1,2,0:T(8,128)S(1)} custom-call(f32[1,128,128]{2,1,0:T(8,128)S(1)} %fusion.201), custom_call_target="InvertDiagBlocksLowerTriangular" | custom-call | tf_op jit(solution)/shard_map/while/body/eval_jaxpr/triangular_solve/custom-call.0 | solution.py:87
  65.9 0.3 bitcast_dynamic-update-slice_fusion.4
  66.2 0.3 fusion.202
  66.5 0.3 convolution_subtract_fusion.4
  66.9 11.7 %cholesky.155 = f32[128,128]{1,0:T(8,128)S(1)} custom-call(f32[128,128]{1,0:T(8,128)S(1)} %fusion.200), custom_call_target="Cholesky" | custom-call | tf_op jit(solution)/shard_map/while/body/eval_jaxpr/jit(cholesky)/cholesky | solution.py:86
  78.6 0.7 compare_reduce_fusion.4
  79.3 0.7 fusion.201
  80.0 9.8 %custom-call.12 = f32[1,128,128]{1,2,0:T(8,128)S(1)} custom-call(f32[1,128,128]{2,1,0:T(8,128)S(1)} %fusion.201), custom_call_target="InvertDiagBlocksLowerTriangular" | custom-call | tf_op jit(solution)/shard_map/while/body/eval_jaxpr/triangular_solve/custom-call.0 | solution.py:87
  89.8 0.3 bitcast_dynamic-update-slice_fusion.4
  90.1 0.3 fusion.202
  90.4 0.3 convolution_subtract_fusion.4
  92.1 0.8 broadcast_in_dim.90
  92.9 7.8 %all-to-all-start.1 = ((f32[256,1,256]{2,1,0:T(1,128)}), f32[256,1,256]{2,1,0:T(1,128)S(1)}, u32[]{:S(2)}, u32[]{:S(2)}) async-start(f32[256,1,256]{2,1,0:T(1,128)} %broadcast_in_dim.90), calls=%async_computation.1 | async-start | bytes 524288 | tf_op jit(solution)/shard_map/all_to_all | solution.py:175
  100.9 0.7 convolution_add_fusion.2
  101.6 47.7 %while.37 = (s32[]{:T(128)}, f32[128,128]{1,0:T(8,128)S(1)}, f32[2,128,128]{2,1,0:T(8,128)S(1)}, f32[128,128]{0,1:T(8,128)S(1)}, f32[128,128]{1,0:T(8,128)S(1)},...) while((s32[]{:T(128)}, f32[128,128]{1,0:T(8,128)S(1)}, f32[2,128,128]{2,1,0:T(8,128)S(1)}, ...), condition=%wide.region_15.18_spmd.clone, body=%wide.region_14.17_spmd.clone.sunk | while | flops 75726976 | bytes 1180773 | solution.py:96
  101.8 11.7 %cholesky.169 = f32[128,128]{1,0:T(8,128)S(1)} custom-call(f32[128,128]{1,0:T(8,128)S(1)} %fusion.207), custom_call_target="Cholesky" | custom-call | tf_op jit(solution)/shard_map/while/body/eval_jaxpr/jit(cholesky)/cholesky | solution.py:86
  113.5 0.6 compare_reduce_fusion.5
  114.2 0.7 fusion.208
  114.8 9.8 %custom-call.13 = f32[1,128,128]{1,2,0:T(8,128)S(1)} custom-call(f32[1,128,128]{2,1,0:T(8,128)S(1)} %fusion.208), custom_call_target="InvertDiagBlocksLowerTriangular" | custom-call | tf_op jit(solution)/shard_map/while/body/eval_jaxpr/triangular_solve/custom-call.0 | solution.py:87
  124.6 0.3 bitcast_dynamic-update-slice_fusion.5
  124.9 0.3 fusion.209
  125.2 0.3 convolution_subtract_fusion.5
  125.6 11.7 %cholesky.169 = f32[128,128]{1,0:T(8,128)S(1)} custom-call(f32[128,128]{1,0:T(8,128)S(1)} %fusion.207), custom_call_target="Cholesky" | custom-call | tf_op jit(solution)/shard_map/while/body/eval_jaxpr/jit(cholesky)/cholesky | solution.py:86
  137.4 0.6 compare_reduce_fusion.5
  138.0 0.7 fusion.208
  138.7 9.8 %custom-call.13 = f32[1,128,128]{1,2,0:T(8,128)S(1)} custom-call(f32[1,128,128]{2,1,0:T(8,128)S(1)} %fusion.208), custom_call_target="InvertDiagBlocksLowerTriangular" | custom-call | tf_op jit(solution)/shard_map/while/body/eval_jaxpr/triangular_solve/custom-call.0 | solution.py:87
  148.5 0.3 bitcast_dynamic-update-slice_fusion.5
  148.8 0.3 fusion.209
  149.1 0.3 convolution_subtract_fusion.5
  149.4 0.5 fusion.46
  150.4 0.7 fusion.27
  151.2 0.5 fusion.28
  151.8 0.5 fusion.61
  153.6 0.5 fusion.51
  154.4 0.8 pad_maximum_fusion.6
  155.2 13.7 %all-to-all-start.2 = ((f32[256,1,80]{2,1,0:T(1,128)}), f32[256,1,80]{2,1,0:T(1,128)S(1)}, u32[]{:S(2)}, u32[]{:S(2)}) async-start(f32[256,1,80]{2,1,0:T(1,128)} %bitcast.48), calls=%async_computation.2 | async-start | bytes 262144 | tf_op jit(solution)/shard_map/all_to_all | solution.py:129
  169.0 11.3 %all-to-all-done.2 = f32[256,1,80]{2,1,0:T(1,128)S(1)} async-done(((f32[256,1,80]{2,1,0:T(1,128)}), f32[256,1,80]{2,1,0:T(1,128)S(1)}, u32[]{:S(2)}, u32[]{:S(2)}) %all-to-all-start.2) | async-done | bytes 81952 | tf_op jit(solution)/shard_map/all_to_all | solution.py:129
  180.4 0.4 fusion.29
  180.9 0.5 fusion.30
  181.3 0.6 pad_maximum_fusion.8
  181.9 0.6 pad_maximum_fusion.7
  (84 shorter events, 6.3 us)
Async XLA Ops:
  0.6 21.2 %copy-start = (f32[223,32]{0,1:T(8,128)S(1)}, f32[223,32]{0,1:T(8,128)}, u32[]{:S(2)}) copy-start(f32[223,32]{0,1:T(8,128)} %param.16) | copy-start | bytes 85636
  4.1 1.0 copy-start.3
  4.1 1.0 copy-start.4
  4.1 1.0 copy-start.5
  9.6 25.4 %all-to-all-start = ((f32[64,1,1048]{2,1,0:T(1,128)}), f32[64,1,1048]{2,1,0:T(1,128)S(1)}, u32[]{:S(2)}, u32[]{:S(2)}) async-start(f32[64,1,1048]{2,1,0:T(1,128)} %all_to_all.27), calls=%async_computation | async-start | bytes 589824 | tf_op jit(solution)/shard_map/all_to_all | solution.py:58
  40.3 1.9 %copy-start.2 = (f32[512,223]{0,1:T(8,128)S(1)}, f32[512,223]{0,1:T(8,128)}, u32[]{:S(2)}) copy-start(f32[512,223]{0,1:T(8,128)} %convolution_multiply_fusion.2) | copy-start | bytes 1370116
  92.9 58.2 %all-to-all-start.1 = ((f32[256,1,256]{2,1,0:T(1,128)}), f32[256,1,256]{2,1,0:T(1,128)S(1)}, u32[]{:S(2)}, u32[]{:S(2)}) async-start(f32[256,1,256]{2,1,0:T(1,128)} %broadcast_in_dim.90), calls=%async_computation.1 | async-start | bytes 524288 | tf_op jit(solution)/shard_map/all_to_all | solution.py:175
  150.2 1.0 copy-start.1
  155.2 25.1 %all-to-all-start.2 = ((f32[256,1,80]{2,1,0:T(1,128)}), f32[256,1,80]{2,1,0:T(1,128)S(1)}, u32[]{:S(2)}, u32[]{:S(2)}) async-start(f32[256,1,80]{2,1,0:T(1,128)} %bitcast.48), calls=%async_computation.2 | async-start | bytes 262144 | tf_op jit(solution)/shard_map/all_to_all | solution.py:129
